TPU v7x, 512 devices: a whole 4x4x16 slice. The times are simulated.
512 devices in a mesh: dp: 32 (over z, core), seq: 16 (over y, x).
Axes of the slice: x: 4, y: 4, z: 16, core: 2. Of those that a mesh axis runs over, the one named last changes fastest.
Arguments:
- mixer_in: bfloat16 [131072, 2816], P(('dp', 'seq')), parts along dimension 0, may hold values from -92 to 92
- gate_input: bfloat16 [131072, 2560], P(('dp', 'seq')), parts along dimension 0, may hold values from -6 to 6
- step_raw: bfloat16 [131072, 40], P(('dp', 'seq')), parts along dimension 0, may hold values from -6 to 6
- lengths: int32 [96], P('dp'), parts along dimension 0, may hold values from 1 to 2048, 4096 in all
- deal_order: int32 [512], P('dp'), parts along dimension 0, may hold values from 0 to 15, as said below
- conv_weight: float32 [4, 2816], replicated, may hold values from -3 to 3
- conv_bias: float32 [2816], replicated, may hold values from -3 to 3
- step_bias: float32 [40], replicated, may hold values from -4 to -1
- decay_rate: float32 [40], replicated, may hold values from 0.01 to 2
- skip_gain: float32 [40], replicated, may hold values from 0.5 to 1.5
- norm_gain: float32 [2560], replicated, may hold values from 0.5 to 1.5
Outputs:
- mixed_out: bfloat16 [131072, 2560], P(('dp', 'seq')), parts along dimension 0
- final_states: float32 [96, 2560, 128], P('dp', 'seq'), parts along dimension 0
There are 32 independent parts, one for each index of `dp`. A program takes and returns all parts, laid end to end along the dimension named above; an argument that names none is the same for every part. Nothing has to cross between parts.
Inputs may be any that keep to these rules, and one draw needn't show every extreme that they name: The prompt lengths sum to 4096 and the longest is exactly 2048. `deal_order`: every sequence stretch stands in exactly one dealt slot.
All inputs are finite; a program needn't handle non-finite values.
Results may differ from a plain program's by a relative error of at most 0.005.
Values may be sent and summed in bfloat16 or wider, within the bound.
No kernel may reach another device: no remote copies, remote signals or barrier semaphores. Data moves between devices by JAX's collectives and lax.ppermute only.
A program may use at most 128 MiB of HBM per device.

v0:
```python
import jax
import jax.numpy as jnp
from jax import lax
from jax.sharding import PartitionSpec as P

HEADS = 40
HEAD_DIM = 64
STATE = 128
KERNEL = 4
STRETCH = 256
DOCS = 3
INNER = 2560
CHANNELS = 2816


def doc_index(ends, positions):
    return jnp.sum((ends[None, :] <= positions[:, None]).astype(jnp.int32), axis=1)


def body(
    mixer_in,
    gate_input,
    step_raw,
    lengths,
    deal_order,
    conv_weight,
    conv_bias,
    step_bias,
    decay_rate,
    skip_gain,
    norm_gain,
):
    myself = lax.axis_index("seq")
    local_rows = mixer_in.shape[0]
    stretches_here = local_rows // STRETCH
    stretch_total = deal_order.shape[0]
    ends = jnp.cumsum(lengths)
    all_stretches = jnp.arange(stretch_total, dtype=jnp.int32)
    my_stretches = lax.dynamic_slice_in_dim(deal_order, myself * stretches_here, stretches_here)
    lane = jnp.arange(STRETCH, dtype=jnp.int32)
    own_doc = doc_index(
        ends, (my_stretches[:, None] * STRETCH + lane[None, :]).reshape(-1)
    ).reshape(stretches_here, STRETCH)
    prev_own = jnp.where(my_stretches > 0, doc_index(ends, my_stretches * STRETCH - 1), -1)
    blocks_in = mixer_in.reshape(stretches_here, STRETCH, CHANNELS)
    tails = blocks_in[:, STRETCH - (KERNEL - 1) :, :]
    step_blocks = step_raw.reshape(stretches_here, STRETCH, HEADS)
    step = jax.nn.softplus(step_blocks.astype(jnp.float32) + step_bias)
    log_decay = -decay_rate * step
    all_tails, all_steps = (
        lax.all_gather(tails, "seq", axis=0, tiled=True),
        lax.all_gather(step_blocks, "seq", axis=0, tiled=True),
    )
    totals = jnp.sum(
        -decay_rate * jax.nn.softplus(all_steps.astype(jnp.float32) + step_bias), axis=1
    )
    slot_map = (deal_order[:, None] == all_stretches[None, :]).astype(jnp.float32)
    packed_totals = jnp.dot(slot_map.T, totals, precision=lax.Precision.HIGHEST)
    prefix = jnp.cumsum(packed_totals, axis=0)
    base = jnp.concatenate([jnp.zeros((1, HEADS), jnp.float32), prefix[:-1]], 0)
    pick_own = (my_stretches[:, None] == all_stretches[None, :]).astype(jnp.float32)
    base_own = jnp.dot(pick_own, base, precision=lax.Precision.HIGHEST)
    running = base_own[:, None, :] + jnp.cumsum(log_decay, axis=1)
    prev_pick = (deal_order[None, :] == my_stretches[:, None] - 1).astype(jnp.bfloat16)
    prev_rows = jnp.einsum(
        "is,skc->ikc", prev_pick, all_tails, preferred_element_type=jnp.float32
    ).astype(jnp.bfloat16)
    extended = jnp.concatenate([prev_rows, blocks_in], 1)
    lead = (
        my_stretches[:, None] * STRETCH
        - (KERNEL - 1)
        + jnp.arange(KERNEL - 1, dtype=jnp.int32)[None, :]
    ).reshape(-1)
    ext_doc = jnp.concatenate(
        [doc_index(ends, lead).reshape(stretches_here, KERNEL - 1), own_doc], 1
    )
    accum = jnp.zeros((stretches_here, STRETCH, CHANNELS), jnp.float32) + conv_bias
    for offset in range(KERNEL):
        keep = (ext_doc[:, offset : offset + STRETCH] == own_doc).astype(jnp.float32)
        accum = (
            accum
            + conv_weight[offset]
            * extended[:, offset : offset + STRETCH, :].astype(jnp.float32)
            * keep[..., None]
        )
    mixed = jax.nn.silu(accum).astype(jnp.bfloat16)
    values = mixed[..., :INNER]
    input_map = mixed[..., INNER : INNER + STATE]
    output_map = mixed[..., INNER + STATE :]
    scaled = (values.astype(jnp.float32) * jnp.repeat(step, HEAD_DIM, axis=2)).astype(jnp.bfloat16)
    end_weight = jnp.exp(
        jnp.where((own_doc == own_doc[:, -1:])[..., None], running[:, -1:, :] - running, -jnp.inf)
    )
    weighted = (scaled.astype(jnp.float32) * jnp.repeat(end_weight, HEAD_DIM, axis=2)).astype(
        jnp.bfloat16
    )
    states = jnp.einsum("isk,isn->ikn", weighted, input_map, preferred_element_type=jnp.float32)
    source_pick = (deal_order[:, None] == all_stretches[None, :]).astype(jnp.float32)
    source_end = jnp.dot(source_pick, prefix, precision=lax.Precision.HIGHEST)
    source_doc = doc_index(ends, deal_order * STRETCH + STRETCH - 1)
    allowed = (deal_order[None, :] < my_stretches[:, None]) & (
        source_doc[None, :] == prev_own[:, None]
    )
    spans = jnp.exp(
        jnp.where(allowed[..., None], base_own[:, None, :] - source_end[None, :, :], -jnp.inf)
    )
    state_in = jnp.einsum(
        "ick,ckn->ikn",
        jnp.repeat(spans, HEAD_DIM, axis=2),
        lax.all_gather(states, "seq", axis=0, tiled=True),
        precision=lax.Precision.HIGHEST,
    )
    later = lane[:, None] >= lane[None, :]
    direct_gain = jnp.repeat(skip_gain, HEAD_DIM)[None, :]

    def stretch_out(inputs):
        values_c, scaled_c, keys_c, queries_c, running_c, doc_c, base_c, prev_c, state_c = inputs
        scores = jnp.dot(queries_c, keys_c.T, preferred_element_type=jnp.float32)
        same = (doc_c[:, None] == doc_c[None, :]) & later
        spans = running_c.T[:, :, None] - running_c.T[:, None, :]
        mixing = (scores[None] * jnp.exp(jnp.where(same[None], spans, -jnp.inf))).astype(
            jnp.bfloat16
        )
        within = jnp.einsum(
            "hts,shp->thp",
            mixing,
            scaled_c.reshape(STRETCH, HEADS, HEAD_DIM),
            preferred_element_type=jnp.float32,
        ).reshape(STRETCH, INNER)
        readout = jnp.dot(
            queries_c, state_c.astype(jnp.bfloat16).T, preferred_element_type=jnp.float32
        )
        carry_weight = jnp.exp(
            jnp.where((doc_c == prev_c)[:, None], running_c - base_c[None, :], -jnp.inf)
        )
        return (
            within
            + readout * jnp.repeat(carry_weight, HEAD_DIM, axis=1)
            + values_c.astype(jnp.float32) * direct_gain
        )

    outputs = lax.map(
        stretch_out,
        (values, scaled, input_map, output_map, running, own_doc, base_own, prev_own, state_in),
    )
    gated = outputs.reshape(local_rows, INNER) * jax.nn.silu(gate_input.astype(jnp.float32))
    normed = gated * lax.rsqrt(jnp.mean(gated * gated, axis=1, keepdims=True) + 1e-05) * norm_gain
    mixed_out = normed.astype(jnp.bfloat16)
    slot_numbers = jnp.arange(stretches_here, dtype=jnp.int32)

    def one_doc(document):
        last = lax.dynamic_index_in_dim(ends, document, keepdims=False) - 1
        owner = last // STRETCH
        match = my_stretches == owner
        slot = jnp.sum(jnp.where(match, slot_numbers, 0))

        def present():
            within_pos = last - owner * STRETCH
            running_c = lax.dynamic_index_in_dim(running, slot, keepdims=False)
            running_e = lax.dynamic_index_in_dim(running_c, within_pos, keepdims=False)
            doc_c = lax.dynamic_index_in_dim(own_doc, slot, keepdims=False)
            scaled_c = lax.dynamic_index_in_dim(scaled, slot, keepdims=False)
            keys_c = lax.dynamic_index_in_dim(input_map, slot, keepdims=False)
            base_c = lax.dynamic_index_in_dim(base_own, slot, keepdims=False)
            prev_c = lax.dynamic_index_in_dim(prev_own, slot, keepdims=False)
            state_c = lax.dynamic_index_in_dim(state_in, slot, keepdims=False)
            weight = jnp.exp(
                jnp.where((doc_c == document)[:, None], running_e[None, :] - running_c, -jnp.inf)
            )
            final_weighted = (
                scaled_c.astype(jnp.float32) * jnp.repeat(weight, HEAD_DIM, axis=1)
            ).astype(jnp.bfloat16)
            part = jnp.dot(final_weighted.T, keys_c, preferred_element_type=jnp.float32)
            carry_weight = jnp.exp(jnp.where(prev_c == document, running_e - base_c, -jnp.inf))
            return part + jnp.repeat(carry_weight, HEAD_DIM)[:, None] * state_c

        def absent():
            return jnp.zeros((INNER, STATE), jnp.float32)

        return lax.cond(jnp.any(match), present, absent)

    every_doc = jnp.transpose(lax.map(one_doc, jnp.arange(DOCS, dtype=jnp.int32)), (1, 0, 2))
    kept = lax.psum_scatter(
        every_doc.astype(jnp.bfloat16), "seq", scatter_dimension=0, tiled=True
    ).astype(jnp.float32)
    final_states = jnp.transpose(kept, (1, 0, 2))
    return (mixed_out, final_states)


def solution(mesh):
    return jax.shard_map(
        body,
        mesh=mesh,
        in_specs=(
            P(("dp", "seq"), None),
            P(("dp", "seq"), None),
            P(("dp", "seq"), None),
            P("dp"),
            P("dp"),
            P(),
            P(),
            P(),
            P(),
            P(),
            P(),
        ),
        out_specs=(P(("dp", "seq"), None), P("dp", "seq", None)),
        check_vma=False,
    )
```

profile of v0, /device:TPU:2, one launch (start us, length us, event | category | flops | bytes accessed | tf_op | source)
XLA Modules:
  0.0 391.7 jit_solution(15185379277083827339)
XLA Ops:
  7.2 0.7 neg.23
  7.9 26.9 %all-gather = bf16[4096,40]{0,1:T(8,128)(2,1)S(1)} all-gather(bf16[256,40]{0,1:T(8,128)(2,1)} %param.17), channel_id=2, replica_groups=mesh['dp'=32,'seq'=16] {'seq'}, dimensions={0}, use_global_device_ids=true | all-gather | bytes 348160 | tf_op jit(solution)/shard_map/all_gather | solution.py:52
  34.8 0.8 multiply_bitcast_fusion
  35.7 0.6 reduce-window.11
  36.3 0.2 slice_reduce_fusion
  36.5 1.2 dynamic_slice.62
  39.0 0.8 reduce-window.10
  39.9 0.2 convert_reduce_fusion.2
  40.1 0.6 slice.90
  40.8 0.8 slice.76
  41.6 21.6 %all_gather.9 = bf16[16,3,2816]{2,1,0:T(4,128)(2,1)S(1)} all-gather(bf16[1,3,2816]{2,1,0:T(4,128)(2,1)S(1)} %slice.76), channel_id=1, replica_groups=mesh['dp'=32,'seq'=16] {'seq'}, dimensions={0}, use_global_device_ids=true | all-gather | bytes 287232 | tf_op jit(solution)/shard_map/all_gather | solution.py:51
  63.2 0.8 fusion.32
  64.1 1.1 slice_reduce_fusion.5
  65.1 0.2 broadcast_in_dim.178
  65.4 2.1 copy.73
  67.5 0.6 fusion.55
  68.8 0.2 copy.93
  69.0 0.6 fusion.30
  69.6 0.2 fusion.45
  70.1 0.8 fusion.42
  70.8 0.1 broadcast.161
  70.9 0.1 add_bitcast_fusion
  71.1 0.6 slice_reduce_fusion.1
  72.3 0.6 broadcast_compare_fusion.1
  73.0 0.1 fusion.38
  73.1 0.2 broadcast_in_dim.184
  73.3 2.1 copy.78
  75.5 5.9 %multiply_convert_fusion.2 = bf16[1,256,2816]{2,1,0:T(8,128)(2,1)S(1)} fusion(bf16[256,2816]{1,0:T(8,128)(2,1)} %param.15, bf16[1,3,2816]{2,1,0:T(4,128)(2,1)S(1)} %copy.108, bf16[1,256,2816]{2,1,0:T(8,128)(2,1)} %bitcast.153, f32[2816]{0:T(1024)S(1)} %get-tuple-element.357, f32[256]{0:T(256)S(1)} %bitcast.173, f32[2816]{0:T(1024)S(1)} %get-tuple-element.358, ...), kind=kLoop, calls=%fused_computation.33 | loop fusion | flops 20905984 | bytes 4401664 | tf_op jit(solution)/shard_map/convert_element_type | solution.py:86
  81.4 0.4 fusion.17
  81.8 1.9 copy-done.1
  83.7 1.8 fusion.25
  85.5 0.2 reduce-scatter.2.cloned.1.call-start
  85.8 1.4 copy.74
  87.3 0.7 compare_and_fusion
  88.0 0.2 fusion.28
  88.2 146.0 %all-gather.4.cloned.1.call-done = f32[40960,128]{1,0:T(8,128)} async-done(((f32[2560,128]{1,0:T(8,128)}), f32[40960,128]{1,0:T(8,128)}) %all-gather.4.cloned.1.call-update) | async-done | bytes 20971536 | tf_op jit(solution)/shard_map/all_gather | solution.py:110
  234.4 38.9 %fusion.6 = f32[2560,1,128]{2,1,0:T(1,128)S(1)} fusion(f32[16,2560,1]{0,2,1:T(1,128)S(1)} %bitcast.151, f32[16,2560,128]{2,1,0:T(8,128)} %bitcast.147), kind=kOutput, calls=%fused_computation.15 | convolution fusion | flops 62914560 | bytes 22446080 | tf_op jit(solution)/shard_map/ick,ckn->ikn/dot_general | solution.py:107
  273.3 20.2 %while.17 = (s32[]{:T(128)}, bf16[3,2560,128]{2,1,0:T(8,128)(2,1)}, s32[3]{0:T(128)S(1)}, s32[3]{0:T(128)S(1)}, s32[1]{0:T(128)}, /*index=5*/bf16[1,256,2560]{1,...) while((s32[]{:T(128)}, bf16[3,2560,128]{2,1,0:T(8,128)(2,1)}, ...), condition=%wide.region_13.14_spmd, body=%wide.region_10.13_spmd.sunk | while | flops 170742112 | bytes 7442075 | solution.py:182
  273.3 0.6 dynamic_slice.66
  275.8 0.6 dynamic_slice.67
  277.7 4.0 %conditional.2 = (bf16[1,2560,128]{2,1,0:T(8,128)(2,1)S(1)}) conditional(s32[]{:T(128)} %bitcast.143, () %tuple.66, (bf16[1,256,2560]{1,2,0:T(8,128)(2,1)}, s32[]{:T(128)}, s32[1,256]{1,0:T(1,128)S(1)}, s32[]{:T(128)}, s32[]{:T(128)}, /*index=5*/f32[1,256,40]{1,2,0:T(8,128)S(1)}, bf16[1,256,128]{2,1,0:T(8,128)(2,1)S(1)}, s32[1]{0:T(128)}, ...), branch_computations={%region_11.11_spmd, %region_12.12_spmd} | conditional | flops 170742096 | bytes 6130356 | solution.py:180
  277.7 0.2 dynamic-slice_reduce_fusion
  277.9 0.7 compare_reduce_fusion
  278.6 1.7 fusion.1
  281.1 0.5 fusion
  281.7 0.9 constant_dynamic-update-slice_fusion.2
  282.5 0.6 dynamic_slice.66
  285.1 0.6 dynamic_slice.67
  287.0 0.1 conditional.2
  287.1 0.9 constant_dynamic-update-slice_fusion.2
  288.0 0.6 dynamic_slice.66
  290.5 0.6 dynamic_slice.67
  292.4 0.1 conditional.2
  292.5 0.9 constant_dynamic-update-slice_fusion.2
  293.4 0.1 fusion.34
  293.5 1.1 fusion.36
  294.6 5.1 %fusion.8 = f32[40,64,256]{2,1,0:T(8,128)} fusion(bf16[256,40,64]{0,2,1:T(8,128)(2,1)} %bitcast.28, f32[40,256]{1,0:T(8,128)S(1)} %bitcast.154, f32[256,256]{1,0:T(8,128)S(1)} %fusion.36, pred[256,256]{1,0:T(8,128)(4,1)S(1)} %fusion.34), kind=kOutput, calls=%fused_computation.18 | convolution fusion | flops 346030080 | bytes 4300800 | tf_op jit(solution)/shard_map/while/body/eval_jaxpr/hts,shp->thp/dot_general | solution.py:124
  299.7 3.2 copy.80
  303.0 1.7 broadcast_in_dim.192
  304.7 3.4 copy.79
  308.2 4.6 %multiply_reduce_fusion = (f32[256]{0:T(256)S(1)}, f32[256,2560]{1,0:T(8,128)S(1)}) fusion(bf16[256,2560]{1,0:T(8,128)(2,1)S(1)} %copy-done.8, f32[2560]{0:T(1024)S(1)} %mul.239, bf16[1,256,2816]{2,1,0:T(8,128)(2,1)} %copy-done.2, f32[256,2560]{1,0:T(8,128)} %copy.80, f32[256,2560]{1,0:T(8,128)} %copy.79, f32[2560,128]{1,0:T(8,128)S(1)} %bitcast.146), kind=kOutput, calls=%fused_computation.40 | convolution fusion | flops 176619264 | bytes 11873280 | tf_op jit(solution)/shard_map/while/body/eval_jaxpr/dot_general | solution.py:130
  312.9 1.3 multiply_convert_fusion.3
  314.2 69.0 %reduce-scatter.2.cloned.1.call-done = bf16[160,3,128]{2,0,1:T(8,128)(2,1)} async-done(((bf16[2560,3,128]{2,0,1:T(8,128)(2,1)}), bf16[160,3,128]{2,0,1:T(8,128)(2,1)}) %reduce-scatter.2.cloned.1.call-update) | async-done | bytes 122896 | tf_op jit(solution)/shard_map/reduce_scatter | solution.py:183
  383.3 1.6 convert_bitcast_fusion.2
  (51 shorter events, 1.5 us)
Async XLA Ops:
  7.2 227.1 %all-gather.4.cloned.1.call-start = ((), (), s32[]{:S(2)}) async-start(), calls=%async_computation.2 | async-start | bytes 22282240 | tf_op jit(solution)/shard_map/all_gather | solution.py:110
  65.4 3.7 copy-start.6
  67.5 2.1 copy-start.5
  73.3 2.1 copy-start.4
  75.5 5.9 %copy-start = (f32[1,256,2560]{2,1,0:T(8,128)S(1)}, f32[1,256,2560]{2,1,0:T(8,128)}, u32[]{:S(2)}) copy-start(f32[1,256,2560]{2,1,0:T(8,128)} %copy.73) | copy-start | bytes 7864324
  81.4 153.0 %copy-start.2 = (bf16[1,256,2816]{2,1,0:T(8,128)(2,1)}, bf16[1,256,2816]{2,1,0:T(8,128)(2,1)S(1)}, u32[]{:S(2)}) copy-start(bf16[1,256,2816]{2,1,0:T(8,128)(2,1)S(1)} %multiply_convert_fusion.2) | copy-start | bytes 4325380
  81.4 2.3 copy-start.1
  85.5 297.7 %reduce-scatter.2.cloned.1.call-start = ((), (), s32[]{:S(2)}) async-start(), calls=%async_computation.1 | async-start | bytes 2088960 | tf_op jit(solution)/shard_map/reduce_scatter | solution.py:183
  304.7 3.4 copy-start.7
  304.7 3.5 copy-start.8
  308.2 4.7 %copy-start.3 = (f32[2560]{0:T(1024)S(1)}, f32[2560]{0:T(1024)}, u32[]{:S(2)}) copy-start(f32[2560]{0:T(1024)} %param.25) | copy-start | bytes 30724
Sparse Core Ops, SparseCore 0:
  85.7 148.5 all-gather.3
  293.6 89.6 reduce-scatter.1
where the time goes:
time: 393 us; the launch traced here: 392 us
  waiting for transfers between devices  215 us (55%)
  matrix products  54 us (14%)
  blocking collectives  48.5 us (12%)
  local copies, waits for them, and re-layouts  28.5 us (7%)
  other arithmetic  18 us (5%)
  between operations  17 us (4%)
  loops' own time  10.3 us (3%)
    all_gather x1, waiting for transfers between devices, body(): lax.all_gather(states, 'seq', axis=0, tiled=True)  146 us
    reduce_scatter x1, waiting for transfers between devices, body(): lax.psum_scatter(every_doc.astype(jnp.bfloat16), 'seq', scatter_dimension...  69 us
    dot_general x1, matrix products, body(): jnp.einsum('ick,ckn->ikn', jnp.repeat(spans, HEAD_DIM, axis=2), lax.all_g...  38.9 us
    all_gather x1, blocking collectives, body(): lax.all_gather(step_blocks, 'seq', axis=0, tiled=True)  26.9 us
    all_gather x1, blocking collectives, body(): lax.all_gather(tails, 'seq', axis=0, tiled=True)  21.6 us
    another operation x1, loops' own time, body(): lax.map(one_doc, jnp.arange(DOCS, dtype=jnp.int32))  9.57 us
  transfers between devices with their start and end apart: 2, of which 2 were waited for; matrix products, arithmetic and copies ran while one was open for 6% of the time, Pallas kernels for 0%

commit v1 on v0

--- a/solution.py
+++ b/solution.py
@@ -11,6 +11,24 @@
 DOCS = 3
 INNER = 2560
 CHANNELS = 2816
+
+
+def note_record_over_axis(a0):
+    vals = []
+    n_all = lax.axis_size("seq")
+    for to_i in [*range(n_all)]:
+        vals.append((to_i, (to_i + 1) % n_all))
+    entries = []
+    for to_i in tuple(range(n_all)):
+        entries.append((to_i, (to_i - 1) % n_all))
+    placed, y = ([a0], [a0])
+    for _ in range(n_all // 2):
+        placed.append(lax.ppermute(placed[-1], axis_name="seq", perm=vals))
+    for _ in [*range((n_all - 1) // 2)]:
+        y.append(lax.ppermute(y[-1], axis_name="seq", perm=entries))
+    arr_now = jnp.concatenate([*placed[::-1], *y[1:]], 0)
+    built = jnp.roll(arr_now, (lax.axis_index("seq") - n_all // 2) * a0.shape[0], 0)
+    return built
 
 
 def doc_index(ends, positions):
@@ -49,7 +67,7 @@
     log_decay = -decay_rate * step
     all_tails, all_steps = (
         lax.all_gather(tails, "seq", axis=0, tiled=True),
-        lax.all_gather(step_blocks, "seq", axis=0, tiled=True),
+        note_record_over_axis(step_blocks),
     )
     totals = jnp.sum(
         -decay_rate * jax.nn.softplus(all_steps.astype(jnp.float32) + step_bias), axis=1

time: 393 us -> 443 us (1.13)
  starting transfers between devices: 0.26 us -> 63.7 us
  blocking collectives: 48.5 us -> 26.3 us
    ppermute x0 -> x15, starting transfers between devices: none -> 63.4 us  [the longest x7 41.9 us: note_record_over_axis(): y.append(lax.ppermute(y[-1], axis_name='seq', perm=entries))]
    all_gather x1 -> x0, blocking collectives: 26.9 us -> none  [body(): lax.all_gather(step_blocks, 'seq', axis=0, tiled=True)]
    all_gather x1, blocking collectives: 21.6 us -> 26.3 us  [body(): lax.all_gather(tails, 'seq', axis=0, tiled=True)]
  transfers between devices with their start and end apart: 2 -> 17, of which waited for: 2 -> 3; matrix products, arithmetic and copies ran while one was open for 6% -> 10% of each run, Pallas kernels for 0% -> 0%
where the time goes in v1:
time: 443 us; the launch traced here: 442 us
  waiting for transfers between devices  219 us (49%)
  starting transfers between devices  63.7 us (14%)
  matrix products  55.3 us (12%)
  local copies, waits for them, and re-layouts  29.9 us (7%)
  blocking collectives  26.3 us (6%)
  other arithmetic  19.5 us (4%)
  between operations  17.4 us (4%)
  loops' own time  10.3 us (2%)
    all_gather x1, waiting for transfers between devices, body(): lax.all_gather(states, 'seq', axis=0, tiled=True)  149 us
    reduce_scatter x1, waiting for transfers between devices, body(): lax.psum_scatter(every_doc.astype(jnp.bfloat16), 'seq', scatter_dimension...  69.5 us
    ppermute x7, starting transfers between devices, note_record_over_axis(): y.append(lax.ppermute(y[-1], axis_name='seq', perm=entries))  41.9 us
    dot_general x1, matrix products, body(): jnp.einsum('ick,ckn->ikn', jnp.repeat(spans, HEAD_DIM, axis=2), lax.all_g...  38.9 us
    all_gather x1, blocking collectives, body(): lax.all_gather(tails, 'seq', axis=0, tiled=True)  26.3 us
    ppermute x8, starting transfers between devices, note_record_over_axis(): placed.append(lax.ppermute(placed[-1], axis_name='seq', perm=vals))  21.5 us
    another operation x1, loops' own time, body(): lax.map(one_doc, jnp.arange(DOCS, dtype=jnp.int32))  9.57 us
  transfers between devices with their start and end apart: 17, of which 3 were waited for; matrix products, arithmetic and copies ran while one was open for 10% of the time, Pallas kernels for 0%

profile of v1, /device:TPU:2, one launch (start us, length us, event | category | flops | bytes accessed | tf_op | source)
XLA Modules:
  0.0 441.8 jit_solution(11050842148515426330)
XLA Ops:
  7.2 3.4 collective-permute-start
  10.6 6.3 %collective-permute-start.8 = (bf16[1,256,40]{1,2,0:T(8,128)(2,1)}, bf16[1,256,40]{1,2,0:T(8,128)(2,1)S(1)}, u32[]{:S(2)}, u32[]{:S(2)}) collective-permute-start(bf16[1,256,40]{1,2,0:T(8,128)(2,1)} %bitcast.157), channel_id=1, source_target_pairs={{0,15},{1,0},{2,1},{3,2},{4,3},{5,4},{6,5},{7,6},{8,7},{9,8},{10,9... | collective-permute-start | bytes 61448 | tf_op jit(solution)/shard_map/ppermute | solution.py:28
  16.9 0.8 reduce-window.10
  17.8 1.2 dynamic_slice.66
  20.6 0.8 slice.76
  21.5 26.3 %all_gather.6 = bf16[16,3,2816]{2,1,0:T(4,128)(2,1)S(1)} all-gather(bf16[1,3,2816]{2,1,0:T(4,128)(2,1)S(1)} %slice.76), channel_id=1, replica_groups=mesh['dp'=32,'seq'=16] {'seq'}, dimensions={0}, use_global_device_ids=true | all-gather | bytes 287232 | tf_op jit(solution)/shard_map/all_gather | solution.py:69
  47.8 0.8 fusion.32
  48.6 1.1 slice_reduce_fusion.5
  49.8 1.9 collective-permute-start.1
  51.7 6.7 %multiply_convert_fusion.2 = bf16[1,256,2816]{2,1,0:T(8,128)(2,1)} fusion(bf16[256,2816]{1,0:T(8,128)(2,1)} %param.15, bf16[1,3,2816]{2,1,0:T(4,128)(2,1)S(1)} %copy.107, bf16[1,256,2816]{2,1,0:T(8,128)(2,1)} %bitcast.152, f32[2816]{0:T(1024)S(1)} %get-tuple-element.357, f32[256]{0:T(256)S(1)} %bitcast.172, f32[2816]{0:T(1024)S(1)} %get-tuple-element.358, ...), kind=kLoop, calls=%fused_computation.33 | loop fusion | flops 20905984 | bytes 4401664 | tf_op jit(solution)/shard_map/convert_element_type | solution.py:104
  58.4 4.5 %collective-permute-start.2 = (bf16[1,256,40]{1,2,0:T(8,128)(2,1)S(1)}, bf16[1,256,40]{1,2,0:T(8,128)(2,1)S(1)}, u32[]{:S(2)}, u32[]{:S(2)}) collective-permute-start(bf16[1,256,40]{1,2,0:T(8,128)(2,1)S(1)} %collective-permute-done.1), channel_id=1, source_target_pairs={{0,1},{1,2},{2,3},{3,4},{4,5},{5,6},{6,7},{7,8},{8,9},{9,10},{10,1... | collective-permute-start | bytes 61448 | tf_op jit(solution)/shard_map/ppermute | solution.py:26
  63.3 2.1 copy.73
  65.4 2.0 collective-permute-start.9
  67.5 3.9 collective-permute-start.3
  71.4 2.4 fusion.17
  73.8 0.6 reduce-window.11
  74.4 4.6 %collective-permute-start.10 = (bf16[1,256,40]{1,2,0:T(8,128)(2,1)S(1)}, bf16[1,256,40]{1,2,0:T(8,128)(2,1)S(1)}, u32[]{:S(2)}, u32[]{:S(2)}) collective-permute-start(bf16[1,256,40]{1,2,0:T(8,128)(2,1)S(1)} %collective-permute-done.9), channel_id=1, source_target_pairs={{0,15},{1,0},{2,1},{3,2},{4,3},{5,4},{6,5},{7,6},{8,7},{9,8},{10,9... | collective-permute-start | bytes 61448 | tf_op jit(solution)/shard_map/ppermute | solution.py:28
  79.1 1.9 collective-permute-start.4
  81.2 7.2 %collective-permute-start.11 = (bf16[1,256,40]{1,2,0:T(8,128)(2,1)S(1)}, bf16[1,256,40]{1,2,0:T(8,128)(2,1)S(1)}, u32[]{:S(2)}, u32[]{:S(2)}) collective-permute-start(bf16[1,256,40]{1,2,0:T(8,128)(2,1)S(1)} %collective-permute-done.10), channel_id=1, source_target_pairs={{0,15},{1,0},{2,1},{3,2},{4,3},{5,4},{6,5},{7,6},{8,7},{9,8},{10,9... | collective-permute-start | bytes 61448 | tf_op jit(solution)/shard_map/ppermute | solution.py:28
  88.5 1.9 collective-permute-start.5
  90.4 7.2 %collective-permute-start.12 = (bf16[1,256,40]{1,2,0:T(8,128)(2,1)S(1)}, bf16[1,256,40]{1,2,0:T(8,128)(2,1)S(1)}, u32[]{:S(2)}, u32[]{:S(2)}) collective-permute-start(bf16[1,256,40]{1,2,0:T(8,128)(2,1)S(1)} %collective-permute-done.11), channel_id=1, source_target_pairs={{0,15},{1,0},{2,1},{3,2},{4,3},{5,4},{6,5},{7,6},{8,7},{9,8},{10,9... | collective-permute-start | bytes 61448 | tf_op jit(solution)/shard_map/ppermute | solution.py:28
  97.7 1.9 collective-permute-start.6
  99.6 0.7 fusion.53
  100.3 0.6 slice.90
  102.2 7.2 %collective-permute-start.13 = (bf16[1,256,40]{1,2,0:T(8,128)(2,1)S(1)}, bf16[1,256,40]{1,2,0:T(8,128)(2,1)S(1)}, u32[]{:S(2)}, u32[]{:S(2)}) collective-permute-start(bf16[1,256,40]{1,2,0:T(8,128)(2,1)S(1)} %collective-permute-done.12), channel_id=1, source_target_pairs={{0,15},{1,0},{2,1},{3,2},{4,3},{5,4},{6,5},{7,6},{8,7},{9,8},{10,9... | collective-permute-start | bytes 61448 | tf_op jit(solution)/shard_map/ppermute | solution.py:28
  109.4 1.9 collective-permute-start.7
  111.3 0.7 broadcast_compare_fusion.1
  112.2 7.2 %collective-permute-start.14 = (bf16[1,256,40]{1,2,0:T(8,128)(2,1)S(1)}, bf16[1,256,40]{1,2,0:T(8,128)(2,1)S(1)}, u32[]{:S(2)}, u32[]{:S(2)}) collective-permute-start(bf16[1,256,40]{1,2,0:T(8,128)(2,1)S(1)} %collective-permute-done.13), channel_id=1, source_target_pairs={{0,15},{1,0},{2,1},{3,2},{4,3},{5,4},{6,5},{7,6},{8,7},{9,8},{10,9... | collective-permute-start | bytes 61448 | tf_op jit(solution)/shard_map/ppermute | solution.py:28
  119.6 1.3 collective-permute-done.14
  121.0 0.6 fusion.30
  121.6 0.3 fusion.44
  121.9 0.8 fusion.42
  122.9 0.6 slice_reduce_fusion.1
  123.7 1.7 broadcast_in_dim.184
  125.4 3.2 copy.78
  128.6 3.5 fusion.25
  132.4 1.4 copy.74
  133.8 0.8 slice.87
  134.8 0.7 compare_and_fusion
  135.7 148.5 %all-gather.3.cloned.1.call-done = f32[40960,128]{1,0:T(8,128)} async-done(((f32[2560,128]{1,0:T(8,128)}), f32[40960,128]{1,0:T(8,128)}) %all-gather.3.cloned.1.call-update) | async-done | bytes 20971536 | tf_op jit(solution)/shard_map/all_gather | solution.py:128
  284.3 38.9 %fusion.6 = f32[2560,1,128]{2,1,0:T(1,128)S(1)} fusion(f32[16,2560,1]{0,2,1:T(1,128)S(1)} %bitcast.150, f32[16,2560,128]{2,1,0:T(8,128)} %bitcast.146), kind=kOutput, calls=%fused_computation.15 | convolution fusion | flops 62914560 | bytes 22446080 | tf_op jit(solution)/shard_map/ick,ckn->ikn/dot_general | solution.py:125
  323.2 20.1 %while.17 = (s32[]{:T(128)}, bf16[3,2560,128]{2,1,0:T(8,128)(2,1)}, s32[3]{0:T(128)S(1)}, s32[3]{0:T(128)S(1)}, s32[1]{0:T(128)}, /*index=5*/bf16[1,256,2560]{1,...) while((s32[]{:T(128)}, bf16[3,2560,128]{2,1,0:T(8,128)(2,1)}, ...), condition=%wide.region_13.14_spmd, body=%wide.region_10.13_spmd.sunk | while | flops 170742112 | bytes 7442075 | solution.py:200
  323.2 0.6 dynamic_slice.72
  325.7 0.6 dynamic_slice.73
  327.6 4.0 conditional.2
  327.8 0.7 compare_reduce_fusion
  328.6 1.7 fusion.1
  331.1 0.5 fusion
  331.6 0.9 constant_dynamic-update-slice_fusion.34
  332.5 0.6 dynamic_slice.72
  335.0 0.6 dynamic_slice.73
  337.0 0.9 constant_dynamic-update-slice_fusion.34
  337.9 0.6 dynamic_slice.72
  340.4 0.6 dynamic_slice.73
  342.4 0.9 constant_dynamic-update-slice_fusion.34
  343.6 1.1 fusion.36
  344.8 1.7 broadcast_in_dim.192
  346.5 3.2 copy.79
  349.7 4.8 %fusion.8 = f32[40,64,256]{2,1,0:T(8,128)} fusion(bf16[256,40,64]{0,2,1:T(8,128)(2,1)} %bitcast.28, f32[40,256]{1,0:T(8,128)S(1)} %bitcast.153, f32[256,256]{1,0:T(8,128)S(1)} %fusion.36, pred[256,256]{1,0:T(8,128)(4,1)S(1)} %fusion.34), kind=kOutput, calls=%fused_computation.18 | convolution fusion | flops 346030080 | bytes 4300800 | tf_op jit(solution)/shard_map/while/body/eval_jaxpr/hts,shp->thp/dot_general | solution.py:142
  354.5 3.4 copy.80
  357.9 4.6 %multiply_reduce_fusion = (f32[256]{0:T(256)S(1)}, f32[256,2560]{1,0:T(8,128)S(1)}) fusion(bf16[256,2560]{1,0:T(8,128)(2,1)S(1)} %copy-done.5, f32[2560]{0:T(1024)S(1)} %mul.239, bf16[1,256,2816]{2,1,0:T(8,128)(2,1)} %multiply_convert_fusion.2, f32[256,2560]{1,0:T(8,128)} %copy.80, f32[256,2560]{1,0:T(8,128)} %copy.79, f32[2560,128]{1,0:T(8,128)S(1)} %bitcast.145), kind=kOutput, calls=%fused_computation.40 | convolution fusion | flops 176619264 | bytes 11873280 | tf_op jit(solution)/shard_map/while/body/eval_jaxpr/dot_general | solution.py:148
  362.5 1.3 multiply_convert_fusion.3
  363.8 69.5 %reduce-scatter.2.cloned.1.call-done = bf16[160,3,128]{2,0,1:T(8,128)(2,1)} async-done(((bf16[2560,3,128]{2,0,1:T(8,128)(2,1)}), bf16[160,3,128]{2,0,1:T(8,128)(2,1)}) %reduce-scatter.2.cloned.1.call-update) | async-done | bytes 122896 | tf_op jit(solution)/shard_map/reduce_scatter | solution.py:201
  433.3 1.6 convert_bitcast_fusion.2
  (106 shorter events, 3.5 us)
Async XLA Ops:
  7.2 277.0 %all-gather.3.cloned.1.call-start = ((), (), s32[]{:S(2)}) async-start(), calls=%async_computation.2 | async-start | bytes 22282240 | tf_op jit(solution)/shard_map/all_gather | solution.py:128
  7.2 42.5 %collective-permute-start = (bf16[1,256,40]{1,2,0:T(8,128)(2,1)}, bf16[1,256,40]{1,2,0:T(8,128)(2,1)S(1)}, u32[]{:S(2)}, u32[]{:S(2)}) collective-permute-start(bf16[1,256,40]{1,2,0:T(8,128)(2,1)} %bitcast.156), channel_id=1, source_target_pairs={{0,1},{1,2},{2,3},{3,4},{4,5},{5,6},{6,7},{7,8},{8,9},{9,10},{10,1... | collective-permute-start | bytes 61448 | tf_op jit(solution)/shard_map/ppermute | solution.py:26
  10.6 54.8 %collective-permute-start.8 = (bf16[1,256,40]{1,2,0:T(8,128)(2,1)}, bf16[1,256,40]{1,2,0:T(8,128)(2,1)S(1)}, u32[]{:S(2)}, u32[]{:S(2)}) collective-permute-start(bf16[1,256,40]{1,2,0:T(8,128)(2,1)} %bitcast.157), channel_id=1, source_target_pairs={{0,15},{1,0},{2,1},{3,2},{4,3},{5,4},{6,5},{7,6},{8,7},{9,8},{10,9... | collective-permute-start | bytes 61448 | tf_op jit(solution)/shard_map/ppermute | solution.py:28
  21.4 37.0 %copy-start.6 = (f32[40]{0:T(128)S(1)}, f32[40]{0:T(128)}, u32[]{:S(2)}) copy-start(f32[40]{0:T(128)} %param.23) | copy-start | bytes 484
  21.4 41.6 %copy-start = (bf16[256,40]{0,1:T(8,128)(2,1)S(1)}, bf16[256,40]{0,1:T(8,128)(2,1)}, u32[]{:S(2)}) copy-start(bf16[256,40]{0,1:T(8,128)(2,1)} %param.17) | copy-start | bytes 61444
  21.4 41.6 %copy-start.3 = (f32[40]{0:T(128)S(1)}, f32[40]{0:T(128)}, u32[]{:S(2)}) copy-start(f32[40]{0:T(128)} %param.22) | copy-start | bytes 484
  49.8 8.7 %collective-permute-start.1 = (bf16[1,256,40]{1,2,0:T(8,128)(2,1)S(1)}, bf16[1,256,40]{1,2,0:T(8,128)(2,1)S(1)}, u32[]{:S(2)}, u32[]{:S(2)}) collective-permute-start(bf16[1,256,40]{1,2,0:T(8,128)(2,1)S(1)} %collective-permute-done), channel_id=1, source_target_pairs={{0,1},{1,2},{2,3},{3,4},{4,5},{5,6},{6,7},{7,8},{8,9},{9,10},{10,1... | collective-permute-start | bytes 61448 | tf_op jit(solution)/shard_map/ppermute | solution.py:26
  58.4 9.0 %collective-permute-start.2 = (bf16[1,256,40]{1,2,0:T(8,128)(2,1)S(1)}, bf16[1,256,40]{1,2,0:T(8,128)(2,1)S(1)}, u32[]{:S(2)}, u32[]{:S(2)}) collective-permute-start(bf16[1,256,40]{1,2,0:T(8,128)(2,1)S(1)} %collective-permute-done.1), channel_id=1, source_target_pairs={{0,1},{1,2},{2,3},{3,4},{4,5},{5,6},{6,7},{7,8},{8,9},{9,10},{10,1... | collective-permute-start | bytes 61448 | tf_op jit(solution)/shard_map/ppermute | solution.py:26
  65.4 56.2 %copy-start.2 = (s32[16]{0:T(128)S(1)}, s32[16]{0:T(128)}, u32[]{:S(2)}) copy-start(s32[16]{0:T(128)} %param.19) | copy-start | bytes 196
  65.4 9.0 %collective-permute-start.9 = (bf16[1,256,40]{1,2,0:T(8,128)(2,1)S(1)}, bf16[1,256,40]{1,2,0:T(8,128)(2,1)S(1)}, u32[]{:S(2)}, u32[]{:S(2)}) collective-permute-start(bf16[1,256,40]{1,2,0:T(8,128)(2,1)S(1)} %collective-permute-done.8), channel_id=1, source_target_pairs={{0,15},{1,0},{2,1},{3,2},{4,3},{5,4},{6,5},{7,6},{8,7},{9,8},{10,9... | collective-permute-start | bytes 61448 | tf_op jit(solution)/shard_map/ppermute | solution.py:28
  67.5 11.6 %collective-permute-start.3 = (bf16[1,256,40]{1,2,0:T(8,128)(2,1)S(1)}, bf16[1,256,40]{1,2,0:T(8,128)(2,1)S(1)}, u32[]{:S(2)}, u32[]{:S(2)}) collective-permute-start(bf16[1,256,40]{1,2,0:T(8,128)(2,1)S(1)} %collective-permute-done.2), channel_id=1, source_target_pairs={{0,1},{1,2},{2,3},{3,4},{4,5},{5,6},{6,7},{7,8},{8,9},{9,10},{10,1... | collective-permute-start | bytes 61448 | tf_op jit(solution)/shard_map/ppermute | solution.py:26
  74.4 6.8 %collective-permute-start.10 = (bf16[1,256,40]{1,2,0:T(8,128)(2,1)S(1)}, bf16[1,256,40]{1,2,0:T(8,128)(2,1)S(1)}, u32[]{:S(2)}, u32[]{:S(2)}) collective-permute-start(bf16[1,256,40]{1,2,0:T(8,128)(2,1)S(1)} %collective-permute-done.9), channel_id=1, source_target_pairs={{0,15},{1,0},{2,1},{3,2},{4,3},{5,4},{6,5},{7,6},{8,7},{9,8},{10,9... | collective-permute-start | bytes 61448 | tf_op jit(solution)/shard_map/ppermute | solution.py:28
  79.1 9.4 %collective-permute-start.4 = (bf16[1,256,40]{1,2,0:T(8,128)(2,1)S(1)}, bf16[1,256,40]{1,2,0:T(8,128)(2,1)S(1)}, u32[]{:S(2)}, u32[]{:S(2)}) collective-permute-start(bf16[1,256,40]{1,2,0:T(8,128)(2,1)S(1)} %collective-permute-done.3), channel_id=1, source_target_pairs={{0,1},{1,2},{2,3},{3,4},{4,5},{5,6},{6,7},{7,8},{8,9},{9,10},{10,1... | collective-permute-start | bytes 61448 | tf_op jit(solution)/shard_map/ppermute | solution.py:26
  81.2 9.2 %collective-permute-start.11 = (bf16[1,256,40]{1,2,0:T(8,128)(2,1)S(1)}, bf16[1,256,40]{1,2,0:T(8,128)(2,1)S(1)}, u32[]{:S(2)}, u32[]{:S(2)}) collective-permute-start(bf16[1,256,40]{1,2,0:T(8,128)(2,1)S(1)} %collective-permute-done.10), channel_id=1, source_target_pairs={{0,15},{1,0},{2,1},{3,2},{4,3},{5,4},{6,5},{7,6},{8,7},{9,8},{10,9... | collective-permute-start | bytes 61448 | tf_op jit(solution)/shard_map/ppermute | solution.py:28
  88.5 9.2 %collective-permute-start.5 = (bf16[1,256,40]{1,2,0:T(8,128)(2,1)S(1)}, bf16[1,256,40]{1,2,0:T(8,128)(2,1)S(1)}, u32[]{:S(2)}, u32[]{:S(2)}) collective-permute-start(bf16[1,256,40]{1,2,0:T(8,128)(2,1)S(1)} %collective-permute-done.4), channel_id=1, source_target_pairs={{0,1},{1,2},{2,3},{3,4},{4,5},{5,6},{6,7},{7,8},{8,9},{9,10},{10,1... | collective-permute-start | bytes 61448 | tf_op jit(solution)/shard_map/ppermute | solution.py:26
  90.4 11.7 %collective-permute-start.12 = (bf16[1,256,40]{1,2,0:T(8,128)(2,1)S(1)}, bf16[1,256,40]{1,2,0:T(8,128)(2,1)S(1)}, u32[]{:S(2)}, u32[]{:S(2)}) collective-permute-start(bf16[1,256,40]{1,2,0:T(8,128)(2,1)S(1)} %collective-permute-done.11), channel_id=1, source_target_pairs={{0,15},{1,0},{2,1},{3,2},{4,3},{5,4},{6,5},{7,6},{8,7},{9,8},{10,9... | collective-permute-start | bytes 61448 | tf_op jit(solution)/shard_map/ppermute | solution.py:28
  97.7 11.7 %collective-permute-start.6 = (bf16[1,256,40]{1,2,0:T(8,128)(2,1)S(1)}, bf16[1,256,40]{1,2,0:T(8,128)(2,1)S(1)}, u32[]{:S(2)}, u32[]{:S(2)}) collective-permute-start(bf16[1,256,40]{1,2,0:T(8,128)(2,1)S(1)} %collective-permute-done.5), channel_id=1, source_target_pairs={{0,1},{1,2},{2,3},{3,4},{4,5},{5,6},{6,7},{7,8},{8,9},{9,10},{10,1... | collective-permute-start | bytes 61448 | tf_op jit(solution)/shard_map/ppermute | solution.py:26
  102.2 10.0 %collective-permute-start.13 = (bf16[1,256,40]{1,2,0:T(8,128)(2,1)S(1)}, bf16[1,256,40]{1,2,0:T(8,128)(2,1)S(1)}, u32[]{:S(2)}, u32[]{:S(2)}) collective-permute-start(bf16[1,256,40]{1,2,0:T(8,128)(2,1)S(1)} %collective-permute-done.12), channel_id=1, source_target_pairs={{0,15},{1,0},{2,1},{3,2},{4,3},{5,4},{6,5},{7,6},{8,7},{9,8},{10,9... | collective-permute-start | bytes 61448 | tf_op jit(solution)/shard_map/ppermute | solution.py:28
  109.4 10.0 %collective-permute-start.7 = (bf16[1,256,40]{1,2,0:T(8,128)(2,1)S(1)}, bf16[1,256,40]{1,2,0:T(8,128)(2,1)S(1)}, u32[]{:S(2)}, u32[]{:S(2)}) collective-permute-start(bf16[1,256,40]{1,2,0:T(8,128)(2,1)S(1)} %collective-permute-done.6), channel_id=1, source_target_pairs={{0,1},{1,2},{2,3},{3,4},{4,5},{5,6},{6,7},{7,8},{8,9},{9,10},{10,1... | collective-permute-start | bytes 61448 | tf_op jit(solution)/shard_map/ppermute | solution.py:26
  112.2 8.7 %collective-permute-start.14 = (bf16[1,256,40]{1,2,0:T(8,128)(2,1)S(1)}, bf16[1,256,40]{1,2,0:T(8,128)(2,1)S(1)}, u32[]{:S(2)}, u32[]{:S(2)}) collective-permute-start(bf16[1,256,40]{1,2,0:T(8,128)(2,1)S(1)} %collective-permute-done.13), channel_id=1, source_target_pairs={{0,15},{1,0},{2,1},{3,2},{4,3},{5,4},{6,5},{7,6},{8,7},{9,8},{10,9... | collective-permute-start | bytes 61448 | tf_op jit(solution)/shard_map/ppermute | solution.py:28
  132.2 301.2 %reduce-scatter.2.cloned.1.call-start = ((), (), s32[]{:S(2)}) async-start(), calls=%async_computation.1 | async-start | bytes 2088960 | tf_op jit(solution)/shard_map/reduce_scatter | solution.py:201
  323.2 20.2 %copy-start.4 = (f32[40]{0:T(128)S(1)}, f32[40]{0:T(128)}, u32[]{:S(2)}) copy-start(f32[40]{0:T(128)} %param.24) | copy-start | bytes 484
  354.5 3.4 copy-start.5
  357.9 4.6 %copy-start.1 = (f32[2560]{0:T(1024)S(1)}, f32[2560]{0:T(1024)}, u32[]{:S(2)}) copy-start(f32[2560]{0:T(1024)} %param.25) | copy-start | bytes 30724
Sparse Core Ops, SparseCore 0:
  132.3 151.8 all-gather.2
  343.5 89.8 reduce-scatter.1
